TPU v7x, 512 devices: a whole 4x8x8 slice. The times are simulated.
512 devices in a mesh: row: 64 (over y, x, core), col: 8 (over z).
Axes of the slice: x: 4, y: 8, z: 8, core: 2. Of those that a mesh axis runs over, the one named last changes fastest.
Arguments:
- panel_cols: float32 [16384, 256], P('row'), may hold values from -60 to 60, as said below
- affinity: float32 [16384, 16384], P('row', 'col'), may hold values from -8 to 8, as said below
Outputs:
- updated: float32 [16384, 16384], P('row', 'col')
- band_block: float32 [256, 256], replicated
Inputs may be any that keep to these rules, and one draw needn't show every extreme that they name: affinity holds a symmetric matrix in the stored column order of the steps. panel_cols has full column rank.
All inputs are finite; a program needn't handle non-finite values.
Results may differ from a plain program's by a relative error of at most 0.000071.
Values sent between devices are 32-bit elements; how exact they have to be, the bound alone decides.
No kernel may reach another device: no remote copies, remote signals or barrier semaphores. Data moves between devices by JAX's collectives and lax.ppermute only.
A program may use at most 64 MiB of HBM per device.

v0:
```python
import jax
import jax.numpy as jnp
from jax import lax
from jax.sharding import PartitionSpec as P


def shards(panel_cols, affinity):
    high = lax.Precision.HIGHEST
    local_rows = panel_cols.shape[0]
    piece_rows = local_rows // lax.axis_size("col")
    col_place = lax.axis_index("col")
    gram_sum = lax.psum(jnp.dot(panel_cols.T, panel_cols, precision=high), "row")
    lower_factor = jnp.linalg.cholesky(gram_sum)
    ortho_basis = jax.scipy.linalg.solve_triangular(lower_factor, panel_cols.T, lower=True).T
    own_basis = lax.dynamic_slice_in_dim(ortho_basis, col_place * piece_rows, piece_rows, 0)
    arrived = lax.all_gather(own_basis, "row", axis=0, tiled=True)
    partial_sum = jnp.dot(affinity, arrived, precision=high)
    partial_sum, basis_cols = (partial_sum, arrived)
    moment = lax.psum(partial_sum, "col")
    band_block = lax.psum(jnp.dot(ortho_basis.T, moment, precision=high), "row")
    corrected = moment - 0.5 * jnp.dot(ortho_basis, band_block, precision=high)
    own_corrected = lax.dynamic_slice_in_dim(corrected, col_place * piece_rows, piece_rows, 0)
    update_cols = lax.all_gather(own_corrected, "row", axis=0, tiled=True)
    updated = affinity - jnp.dot(ortho_basis, update_cols.T, precision=high)
    updated = updated - jnp.dot(corrected, basis_cols.T, precision=high)
    return (updated, band_block)


def solution(mesh):
    placed = (P("row", None), P("row", "col"))
    return jax.shard_map(
        shards, mesh=mesh, in_specs=placed, out_specs=(P("row", "col"), P()), check_vma=False
    )
```

profile of v0, /device:TPU:1, one launch (start us, length us, event | category | flops | bytes accessed | tf_op | source)
XLA Modules:
  0.0 722.9 jit_solution(2886932835697183772)
XLA Ops:
  7.2 2.3 fusion.16
  9.6 196.8 %all-reduce.5.cloned.1.call-done = f32[256,256]{0,1:T(8,128)} async-done(((f32[256,256]{0,1:T(8,128)}), f32[256,256]{0,1:T(8,128)}) %all-reduce.5.cloned.1.call-update) | async-done | bytes 262160 | tf_op jit(solution)/shard_map/psum | solution.py:12
  206.4 1.1 copy.8
  207.5 1.0 fusion.1
  208.5 11.7 %cholesky.50 = f32[128,128]{1,0:T(8,128)S(1)} custom-call(f32[128,128]{1,0:T(8,128)S(1)} %cholesky.118), custom_call_target="Cholesky" | custom-call | tf_op jit(solution)/shard_map/jit(cholesky)/cholesky | solution.py:13
  220.3 9.8 %custom-call.15 = f32[1,128,128]{1,2,0:T(8,128)S(1)} custom-call(f32[1,128,128]{2,1,0:T(8,128)S(1)} %get-tuple-element.23), custom_call_target="InvertDiagBlocksLowerTriangular" | custom-call | tf_op jit(solution)/shard_map/jit(cholesky)/cholesky | solution.py:13
  230.1 0.2 constant_dynamic-update-slice_fusion
  230.3 0.3 convolution_subtract_fusion.3
  230.6 11.7 %cholesky.105 = f32[128,128]{1,0:T(8,128)S(1)} custom-call(f32[128,128]{1,0:T(8,128)S(1)} %convolution_subtract_fusion.3), custom_call_target="Cholesky" | custom-call | tf_op jit(solution)/shard_map/jit(cholesky)/cholesky | solution.py:13
  242.3 0.7 compare_reduce_fusion
  244.4 4.1 while.1
  244.5 0.6 fusion.31
  245.1 1.4 bitcast_dynamic-update-slice_fusion.2
  246.5 0.6 fusion.31
  247.1 1.4 bitcast_dynamic-update-slice_fusion.2
  248.5 19.7 %custom-call.16 = f32[2,128,128]{1,2,0:T(8,128)S(1)} custom-call(f32[2,128,128]{2,1,0:T(8,128)S(1)} %get-tuple-element.9), custom_call_target="InvertDiagBlocksLowerTriangular" | custom-call | tf_op jit(solution)/shard_map/jit(_solve_triangular)/triangular_solve | solution.py:14
  268.1 0.3 fusion.5
  268.5 0.4 convolution_subtract_fusion.2
  268.9 0.3 fusion.8
  269.2 0.1 fusion.4
  269.3 0.7 copy.9
  270.1 80.7 %all-gather.3.cloned.1.call-done = f32[2048,256]{1,0:T(8,128)} async-done(((f32[32,256]{1,0:T(8,128)}), f32[2048,256]{1,0:T(8,128)}) %all-gather.3.cloned.1.call-update) | async-done | bytes 2097168 | tf_op jit(solution)/shard_map/all_gather | solution.py:16
  350.7 4.2 convolution_bitcast_fusion
  355.0 71.6 %all-reduce.7.cloned.1.call-done = f32[256,256]{1,0:T(8,128)} async-done(((f32[256,256]{1,0:T(8,128)}), f32[256,256]{1,0:T(8,128)}) %all-reduce.7.cloned.1.call-update) | async-done | bytes 262160 | tf_op jit(solution)/shard_map/psum | solution.py:19
  426.6 2.0 fusion.2
  428.7 193.9 %all-reduce.9.cloned.1.call-done = f32[256,256]{1,0:T(8,128)} async-done(((f32[256,256]{1,0:T(8,128)}), f32[256,256]{1,0:T(8,128)}) %all-reduce.9.cloned.1.call-update) | async-done | bytes 262160 | tf_op jit(solution)/shard_map/psum | solution.py:20
  622.6 1.6 fusion
  624.2 0.6 constant_dynamic-slice_fusion.1
  624.9 82.1 %all-gather.5.cloned.1.call-done = f32[2048,256]{1,0:T(8,128)} async-done(((f32[32,256]{1,0:T(8,128)}), f32[2048,256]{1,0:T(8,128)}) %all-gather.5.cloned.1.call-update) | async-done | bytes 2097168 | tf_op jit(solution)/shard_map/all_gather | solution.py:23
  707.0 5.3 convolution_subtract_fusion.1
  712.3 3.4 convolution_subtract_fusion
  715.6 0.7 copy.26
  (28 shorter events, 0.5 us)
Async XLA Ops:
  7.2 199.3 %all-reduce.5.cloned.1.call-start = ((), (), s32[]{:S(2)}) async-start(), calls=%async_computation | async-start | bytes 524288 | tf_op jit(solution)/shard_map/psum | solution.py:12
  9.5 258.6 %copy-start.2 = (f32[256,256]{1,0:T(8,128)S(1)}, f32[256,256]{1,0:T(8,128)}, u32[]{:S(2)}) copy-start(f32[256,256]{1,0:T(8,128)} %param.2) | copy-start | bytes 786436
  9.6 341.1 %all-gather.3.cloned.1.call-start = ((), (), s32[]{:S(2)}) async-start(), calls=%async_computation.1 | async-start | bytes 2129920 | tf_op jit(solution)/shard_map/all_gather | solution.py:16
  220.2 130.5 %copy-start = (f32[256,2048]{1,0:T(8,128)S(1)}, f32[256,2048]{1,0:T(8,128)}, u32[]{:S(2)}) copy-start(f32[256,2048]{1,0:T(8,128)} %param.3) | copy-start | bytes 6291460
  270.0 156.6 %all-reduce.7.cloned.1.call-start = ((), (), s32[]{:S(2)}) async-start(), calls=%async_computation.2 | async-start | bytes 524288 | tf_op jit(solution)/shard_map/psum | solution.py:19
  355.0 267.6 %all-reduce.9.cloned.1.call-start = ((), (), s32[]{:S(2)}) async-start(), calls=%async_computation.3 | async-start | bytes 524288 | tf_op jit(solution)/shard_map/psum | solution.py:20
  428.7 278.3 %all-gather.5.cloned.1.call-start = ((), (), s32[]{:S(2)}) async-start(), calls=%async_computation.4 | async-start | bytes 2129920 | tf_op jit(solution)/shard_map/all_gather | solution.py:23
  707.0 5.3 copy-start.1
  712.2 3.4 copy-start.3
Sparse Core Ops, SparseCore 0:
  12.0 194.3 all-reduce.4
  270.1 80.5 all-gather.2
  355.1 71.4 all-reduce.6
  430.5 192.0 all-reduce.8
  626.4 80.5 all-gather.4
where the time goes:
time: 723 us
  waiting for transfers between devices  625 us (86%)
  other arithmetic  54.8 us (8%)
  matrix products  20.3 us (3%)
  between operations  15.2 us (2%)
    psum x1, waiting for transfers between devices, shards(): lax.psum(jnp.dot(panel_cols.T, panel_cols, precision=high), 'row')  197 us
    psum x1, waiting for transfers between devices, shards(): band_block = lax.psum(jnp.dot(ortho_basis.T, moment, precision=high), 'row')  194 us
    all_gather x1, waiting for transfers between devices, shards(): update_cols = lax.all_gather(own_corrected, 'row', axis=0, tiled=True)  82.1 us
    all_gather x1, waiting for transfers between devices, shards(): arrived = lax.all_gather(own_basis, 'row', axis=0, tiled=True)  80.7 us
    psum x1, waiting for transfers between devices, shards(): moment = lax.psum(partial_sum, 'col')  71.6 us
    another operation x6, other arithmetic, shards(): lower_factor = jnp.linalg.cholesky(gram_sum)  34 us
    another operation x3, other arithmetic, shards(): jax.scipy.linalg.solve_triangular(lower_factor, panel_cols.T, lower=True)  19.7 us
  transfers between devices with their start and end apart: 5, of which 5 were waited for; matrix products, arithmetic and copies ran while one was open for 0% of the time, Pallas kernels for 0%

commit v1 on v0

--- a/solution.py
+++ b/solution.py
@@ -17,7 +17,9 @@
     partial_sum = jnp.dot(affinity, arrived, precision=high)
     partial_sum, basis_cols = (partial_sum, arrived)
     moment = lax.psum(partial_sum, "col")
-    band_block = lax.psum(jnp.dot(ortho_basis.T, moment, precision=high), "row")
+    band_block = jnp.sum(
+        lax.all_gather(jnp.dot(ortho_basis.T, moment, precision=high), "row"), axis=0
+    )
     corrected = moment - 0.5 * jnp.dot(ortho_basis, band_block, precision=high)
     own_corrected = lax.dynamic_slice_in_dim(corrected, col_place * piece_rows, piece_rows, 0)
     update_cols = lax.all_gather(own_corrected, "row", axis=0, tiled=True)

time: 723 us -> 642 us (0.89)
  waiting for transfers between devices: 625 us -> 539 us
    psum x1 -> x0, waiting for transfers between devices: 194 us -> none  [shards(): band_block = lax.psum(jnp.dot(ortho_basis.T, moment, precision=high), 'row')]
    all_gather x0 -> x1, waiting for transfers between devices: none -> 110 us  [shards(): lax.all_gather(jnp.dot(ortho_basis.T, moment, precision=high), 'row')]
where the time goes in v1:
time: 642 us
  waiting for transfers between devices  539 us (84%)
  other arithmetic  61.6 us (10%)
  matrix products  19.3 us (3%)
  between operations  15.2 us (2%)
    psum x1, waiting for transfers between devices, shards(): lax.psum(jnp.dot(panel_cols.T, panel_cols, precision=high), 'row')  197 us
    all_gather x1, waiting for transfers between devices, shards(): lax.all_gather(jnp.dot(ortho_basis.T, moment, precision=high), 'row')  110 us
    all_gather x1, waiting for transfers between devices, shards(): arrived = lax.all_gather(own_basis, 'row', axis=0, tiled=True)  80.7 us
    all_gather x1, waiting for transfers between devices, shards(): update_cols = lax.all_gather(own_corrected, 'row', axis=0, tiled=True)  80.3 us
    psum x1, waiting for transfers between devices, shards(): moment = lax.psum(partial_sum, 'col')  71.6 us
    another operation x6, other arithmetic, shards(): lower_factor = jnp.linalg.cholesky(gram_sum)  33.9 us
    another operation x3, other arithmetic, shards(): jax.scipy.linalg.solve_triangular(lower_factor, panel_cols.T, lower=True)  19.7 us
  transfers between devices with their start and end apart: 5, of which 5 were waited for; matrix products, arithmetic and copies ran while one was open for 0% of the time, Pallas kernels for 0%

profile of v1, /device:TPU:1, one launch (start us, length us, event | category | flops | bytes accessed | tf_op | source)
XLA Modules:
  0.0 641.8 jit_solution(11749878021910143240)
XLA Ops:
  7.2 2.4 fusion.16
  9.7 196.7 %all-reduce.4.cloned.1.call-done = f32[256,256]{0,1:T(8,128)} async-done(((f32[256,256]{0,1:T(8,128)}), f32[256,256]{0,1:T(8,128)}) %all-reduce.4.cloned.1.call-update) | async-done | bytes 262160 | tf_op jit(solution)/shard_map/psum | solution.py:12
  206.4 1.1 copy.8
  207.5 1.0 fusion.1
  208.5 11.7 %cholesky.50 = f32[128,128]{1,0:T(8,128)S(1)} custom-call(f32[128,128]{1,0:T(8,128)S(1)} %cholesky.118), custom_call_target="Cholesky" | custom-call | tf_op jit(solution)/shard_map/jit(cholesky)/cholesky | solution.py:13
  220.3 9.8 %custom-call.15 = f32[1,128,128]{1,2,0:T(8,128)S(1)} custom-call(f32[1,128,128]{2,1,0:T(8,128)S(1)} %get-tuple-element.23), custom_call_target="InvertDiagBlocksLowerTriangular" | custom-call | tf_op jit(solution)/shard_map/jit(cholesky)/cholesky | solution.py:13
  230.1 0.2 constant_dynamic-update-slice_fusion
  230.3 0.3 convolution_subtract_fusion.3
  230.6 11.7 %cholesky.105 = f32[128,128]{1,0:T(8,128)S(1)} custom-call(f32[128,128]{1,0:T(8,128)S(1)} %convolution_subtract_fusion.3), custom_call_target="Cholesky" | custom-call | tf_op jit(solution)/shard_map/jit(cholesky)/cholesky | solution.py:13
  242.3 0.6 compare_reduce_fusion
  244.3 4.0 while.1
  244.5 0.6 fusion.31
  245.0 1.3 bitcast_dynamic-update-slice_fusion.2
  246.4 0.6 fusion.31
  247.0 1.3 bitcast_dynamic-update-slice_fusion.2
  248.3 19.7 %custom-call.16 = f32[2,128,128]{1,2,0:T(8,128)S(1)} custom-call(f32[2,128,128]{2,1,0:T(8,128)S(1)} %get-tuple-element.9), custom_call_target="InvertDiagBlocksLowerTriangular" | custom-call | tf_op jit(solution)/shard_map/jit(_solve_triangular)/triangular_solve | solution.py:14
  268.0 0.3 fusion.5
  268.3 0.4 convolution_subtract_fusion.2
  268.7 0.3 fusion.8
  269.0 0.1 fusion.4
  269.1 0.7 copy.9
  269.9 80.7 %all-gather.5.cloned.1.call-done = f32[2048,256]{1,0:T(8,128)} async-done(((f32[32,256]{1,0:T(8,128)}), f32[2048,256]{1,0:T(8,128)}) %all-gather.5.cloned.1.call-update) | async-done | bytes 2097168 | tf_op jit(solution)/shard_map/all_gather | solution.py:16
  350.5 4.2 convolution_bitcast_fusion
  354.8 71.6 %all-reduce.6.cloned.1.call-done = f32[256,256]{1,0:T(8,128)} async-done(((f32[256,256]{1,0:T(8,128)}), f32[256,256]{1,0:T(8,128)}) %all-reduce.6.cloned.1.call-update) | async-done | bytes 262160 | tf_op jit(solution)/shard_map/psum | solution.py:19
  426.4 2.0 fusion.2
  428.5 109.6 %all-gather.9.cloned.1.call-done = f32[16384,256]{1,0:T(8,128)} async-done(((f32[256,256]{1,0:T(8,128)}), f32[16384,256]{1,0:T(8,128)}) %all-gather.9.cloned.1.call-update) | async-done | bytes 16777232 | tf_op jit(solution)/shard_map/all_gather | solution.py:21
  538.1 6.9 %reduce_sum.9 = f32[256,256]{1,0:T(8,128)S(1)} reduce(f32[64,256,256]{2,1,0:T(8,128)} %bitcast.46, f32[]{:T(128)} %constant.83.clone.1), dimensions={0}, to_apply=%region_6.7 | reduce | flops 4128768 | bytes 17039364 | tf_op jit(solution)/shard_map/reduce_sum | solution.py:20
  545.0 0.6 fusion
  545.6 0.6 constant_dynamic-slice_fusion.1
  546.3 80.3 %all-gather.7.cloned.1.call-done = f32[2048,256]{1,0:T(8,128)} async-done(((f32[32,256]{1,0:T(8,128)}), f32[2048,256]{1,0:T(8,128)}) %all-gather.7.cloned.1.call-update) | async-done | bytes 2097168 | tf_op jit(solution)/shard_map/all_gather | solution.py:25
  626.6 5.3 convolution_subtract_fusion.1
  631.9 3.4 convolution_subtract_fusion
  (30 shorter events, 0.5 us)
Async XLA Ops:
  7.2 199.3 %all-reduce.4.cloned.1.call-start = ((), (), s32[]{:S(2)}) async-start(), calls=%async_computation | async-start | bytes 524288 | tf_op jit(solution)/shard_map/psum | solution.py:12
  9.6 258.4 %copy-start.2 = (f32[256,256]{1,0:T(8,128)S(1)}, f32[256,256]{1,0:T(8,128)}, u32[]{:S(2)}) copy-start(f32[256,256]{1,0:T(8,128)} %param.2) | copy-start | bytes 786436
  9.6 340.9 %all-gather.5.cloned.1.call-start = ((), (), s32[]{:S(2)}) async-start(), calls=%async_computation.1 | async-start | bytes 2129920 | tf_op jit(solution)/shard_map/all_gather | solution.py:16
  220.2 130.3 %copy-start = (f32[256,2048]{1,0:T(8,128)S(1)}, f32[256,2048]{1,0:T(8,128)}, u32[]{:S(2)}) copy-start(f32[256,2048]{1,0:T(8,128)} %param.3) | copy-start | bytes 6291460
  269.8 156.6 %all-reduce.6.cloned.1.call-start = ((), (), s32[]{:S(2)}) async-start(), calls=%async_computation.2 | async-start | bytes 524288 | tf_op jit(solution)/shard_map/psum | solution.py:19
  354.8 183.4 %all-gather.9.cloned.1.call-start = ((), (), s32[]{:S(2)}) async-start(), calls=%async_computation.4 | async-start | bytes 17039360 | tf_op jit(solution)/shard_map/all_gather | solution.py:21
  428.5 198.1 %all-gather.7.cloned.1.call-start = ((), (), s32[]{:S(2)}) async-start(), calls=%async_computation.3 | async-start | bytes 2129920 | tf_op jit(solution)/shard_map/all_gather | solution.py:25
  538.1 6.9 %copy-start.4 = (f32[256,256]{1,0:T(8,128)S(1)}, f32[256,256]{1,0:T(8,128)}, u32[]{:S(2)}) copy-start(f32[256,256]{1,0:T(8,128)} %all-reduce.6.cloned.1.call-done) | copy-start | bytes 786436
  545.0 86.8 %copy-start.3 = (f32[256,256]{1,0:T(8,128)}, f32[256,256]{1,0:T(8,128)S(1)}, u32[]{:S(2)}) copy-start(f32[256,256]{1,0:T(8,128)S(1)} %reduce_sum.9) | copy-start | bytes 786436
  626.6 5.3 copy-start.1
Sparse Core Ops, SparseCore 0:
  12.0 194.3 all-reduce.3
  269.9 80.5 all-gather.4
  354.9 71.4 all-reduce.5
  430.2 107.8 all-gather.8
  546.4 80.1 all-gather.6
